TPU v7x, 512 devices: a whole 4x4x16 slice. The times are simulated.
512 devices in a mesh: comp: 32 (over z, core), feat: 16 (over x, y).
Axes of the slice: x: 4, y: 4, z: 16, core: 2. Of those that a mesh axis runs over, the one named last changes fastest.
Arguments:
- block_values: bfloat16 [32, 16, 24, 128, 128], P('comp', 'feat'), may hold values from -0.0625 to 0.0625
- block_rows: int32 [32, 16, 24], P('comp', 'feat'), may hold values from 0 to 15, as said below
- block_cols: int32 [32, 16, 24], P('comp', 'feat'), may hold values from 0 to 13, as said below
- block_counts: int32 [32, 16], P('comp', 'feat'), may hold values from 8 to 24, as said below
- right_side: float32 [65536, 128], P(('comp', 'feat')), may hold values from -6 to 6
- ridge: float32 [128], replicated, may hold values from 0.1 to 2
Outputs:
- solution: float32 [28672, 128], P('feat')
- residual: float32 [65536, 128], P(('comp', 'feat'))
Inputs may be any that keep to these rules, and one draw needn't show every extreme that they name: Within one device the listed (block_rows, block_cols) pairs of all 24 slots are distinct; block rows are very uneven in how many blocks they hold. `block_cols`: see block_rows. `block_counts`: slots at or beyond a device's count are ignored; some device is full in every draw.
All inputs are finite; a program needn't handle non-finite values.
Results may differ from a plain program's by a relative error of at most 0.0029.
Values may be sent and summed in bfloat16 or wider, within the bound.
No kernel may reach another device: no remote copies, remote signals or barrier semaphores. Data moves between devices by JAX's collectives and lax.ppermute only.
A program may use at most 64 MiB of HBM per device.

v0:
```python
import jax
import jax.numpy as jnp
from jax import lax
from jax.sharding import PartitionSpec as P

RB_DEV = 16
CB_DEV = 14
ITERS = 2


def shards(block_values, block_rows, block_cols, block_counts, right_side, ridge):
    values = block_values[0, 0]
    slot_rows = block_rows[0, 0]
    slot_cols = block_cols[0, 0]
    count_of_slots = block_counts[0, 0]
    responses = right_side.shape[1]
    total_slot_number = values.shape[0]
    block_edge = values.shape[1]
    slot_live = (jnp.arange(total_slot_number) < count_of_slots).astype(jnp.float32)
    row_lookup_table = (jnp.arange(RB_DEV)[:, None] == slot_rows[None, :]).astype(
        jnp.float32
    ) * slot_live[None, :]
    col_table = (jnp.arange(CB_DEV)[:, None] == slot_cols[None, :]).astype(jnp.float32) * slot_live[
        None, :
    ]
    first_comp = (lax.axis_index("comp") == 0).astype(jnp.float32)

    def backward(low_slab):
        row_slabs = low_slab.reshape(RB_DEV, block_edge, responses)
        selected = jnp.take(row_slabs, slot_rows, axis=0)
        block_products = jnp.einsum(
            "sij,sik->sjk", values, selected, preferred_element_type=jnp.float32
        )
        summed = jnp.einsum(
            "qs,sjk->qjk", col_table, block_products, precision=lax.Precision.HIGHEST
        )
        return summed.reshape(CB_DEV * block_edge, responses)

    residual = right_side
    image_weight = 1.0

    def slab_of(current):
        return lax.all_gather(current.astype(jnp.bfloat16), "feat", axis=0, tiled=True)

    def reduce_grad(partial_contribution):
        return lax.psum(partial_contribution, "comp")

    def grad_total(gradient):
        return lax.psum(first_comp * jnp.sum(gradient * gradient, axis=0), ("comp", "feat"))

    gradient = reduce_grad(backward(slab_of(residual)))
    energy = grad_total(gradient)
    search_direction = gradient
    solution = jnp.zeros_like(gradient)
    for step_index in range(ITERS):
        col_panels = search_direction.astype(jnp.bfloat16).reshape(CB_DEV, block_edge, responses)
        forward_selected = jnp.take(col_panels, slot_cols, axis=0)
        forward_block_products = jnp.einsum(
            "sij,sjk->sik", values, forward_selected, preferred_element_type=jnp.float32
        )
        forward_summed = jnp.einsum(
            "rs,sik->rik", row_lookup_table, forward_block_products, precision=lax.Precision.HIGHEST
        )
        image_rows = lax.psum_scatter(
            forward_summed.reshape(RB_DEV * block_edge, responses),
            "feat",
            scatter_dimension=0,
            tiled=True,
        )
        image_energy, direction_energy = lax.psum(
            (
                image_weight * jnp.sum(image_rows * image_rows, axis=0),
                first_comp * jnp.sum(search_direction * search_direction, axis=0),
            ),
            ("comp", "feat"),
        )
        step_size = energy / (image_energy + ridge * direction_energy)
        solution = solution + step_size * search_direction
        residual = residual - step_size * image_rows
        if step_index + 1 < ITERS:
            gradient = reduce_grad(backward(slab_of(residual))) - ridge * solution
            next_energy = grad_total(gradient)
            search_direction = gradient + next_energy / energy * search_direction
            energy = next_energy
    return (solution, residual)


def solution(mesh):
    placed = (
        P("comp", "feat", None, None, None),
        P("comp", "feat", None),
        P("comp", "feat", None),
        P("comp", "feat"),
        P(("comp", "feat"), None),
        P(),
    )
    return jax.shard_map(
        shards,
        mesh=mesh,
        in_specs=placed,
        out_specs=(P("feat", None), P(("comp", "feat"), None)),
        check_vma=False,
    )
```

profile of v0, /device:TPU:1, one launch (start us, length us, event | category | flops | bytes accessed | tf_op | source)
XLA Modules:
  0.0 996.0 jit_solution(15830034595637753856)
XLA Ops:
  10.1 20.0 %all_gather.6 = bf16[2048,128]{1,0:T(8,128)(2,1)S(1)} all-gather(bf16[128,128]{1,0:T(8,128)(2,1)S(1)} %convert_element_type.26), channel_id=1, replica_groups=mesh['comp'=32,'feat'=16] {'feat'}, dimensions={0}, use_global_device_ids=true | all-gather | bytes 557056 | tf_op jit(solution)/shard_map/all_gather | solution.py:43
  30.8 1.7 fusion.14
  32.5 2.0 copy.12
  36.8 213.7 %all-reduce.5.cloned.1.call-done = f32[1792,128]{1,0:T(8,128)} async-done(((f32[1792,128]{1,0:T(8,128)}), f32[1792,128]{1,0:T(8,128)}) %all-reduce.5.cloned.1.call-update) | async-done | bytes 917520 | tf_op jit(solution)/shard_map/psum | solution.py:46
  250.5 1.7 multiply_reduce_fusion.2
  253.0 2.0 fusion.12
  255.0 2.0 copy.13
  258.0 1.3 copy.9
  259.4 86.1 %reduce-scatter.3.cloned.1.call-done = f32[128,128]{1,0:T(8,128)} async-done(((f32[2048,128]{1,0:T(8,128)}), f32[128,128]{1,0:T(8,128)}) %reduce-scatter.3.cloned.1.call-update) | async-done | bytes 65552 | tf_op jit(solution)/shard_map/reduce_scatter | solution.py:64
  346.3 105.3 %all-reduce.1 = (f32[128]{0:T(128)S(1)}, f32[128]{0:T(128)S(1)}) all-reduce(f32[128]{0:T(128)S(1)} %broadcast_multiply_fusion.2, f32[128]{0:T(128)S(1)} %multiply_reduce_fusion.4), channel_id=1, replica_groups=mesh['comp'=32,'feat'=16] {'comp','feat'}, use_global_device_ids=true, to_apply=%region_2.4 | all-reduce | flops 256 | bytes 2048 | tf_op jit(solution)/shard_map/psum | solution.py:49
  452.5 16.0 %all_gather.7 = bf16[2048,128]{1,0:T(8,128)(2,1)S(1)} all-gather(bf16[128,128]{1,0:T(8,128)(2,1)S(1)} %fusion.28), channel_id=1, replica_groups=mesh['comp'=32,'feat'=16] {'feat'}, dimensions={0}, use_global_device_ids=true | all-gather | bytes 557056 | tf_op jit(solution)/shard_map/all_gather | solution.py:43
  469.2 1.7 fusion.10
  470.9 2.0 copy.14
  473.9 1.2 copy.10
  475.2 208.0 %all-reduce.7.cloned.1.call-done = f32[1792,128]{1,0:T(8,128)} async-done(((f32[1792,128]{1,0:T(8,128)}), f32[1792,128]{1,0:T(8,128)}) %all-reduce.7.cloned.1.call-update) | async-done | bytes 917520 | tf_op jit(solution)/shard_map/psum | solution.py:46
  683.2 1.5 multiply_reduce_fusion.1
  684.7 105.2 %psum.56 = f32[128]{0:T(128)S(1)} all-reduce(f32[128]{0:T(128)S(1)} %broadcast_multiply_fusion.1), channel_id=1, replica_groups=mesh['comp'=32,'feat'=16] {'comp','feat'}, use_global_device_ids=true, to_apply=%region_8.11 | all-reduce | flops 128 | bytes 1024 | tf_op jit(solution)/shard_map/psum | solution.py:49
  790.2 1.6 gather_fusion.3
  791.7 3.1 fusion.8
  794.8 3.0 copy.15
  797.9 2.4 fusion
  800.3 1.3 copy.11
  801.6 79.8 %reduce-scatter.5.cloned.1.call-done = f32[128,128]{1,0:T(8,128)} async-done(((f32[2048,128]{1,0:T(8,128)}), f32[128,128]{1,0:T(8,128)}) %reduce-scatter.5.cloned.1.call-update) | async-done | bytes 65552 | tf_op jit(solution)/shard_map/reduce_scatter | solution.py:64
  882.4 105.3 %all-reduce = (f32[128]{0:T(128)S(1)}, f32[128]{0:T(128)S(1)}) all-reduce(f32[128]{0:T(128)S(1)} %multiply_reduce_fusion.3, f32[128]{0:T(128)S(1)} %broadcast_multiply_fusion), channel_id=1, replica_groups=mesh['comp'=32,'feat'=16] {'comp','feat'}, use_global_device_ids=true, to_apply=%region_11.14 | all-reduce | flops 256 | bytes 2048 | tf_op jit(solution)/shard_map/psum | solution.py:70
  (53 shorter events, 13.6 us)
Async XLA Ops:
  7.2 23.6 %copy-start = (bf16[1,1,24,128,128]{4,3,2,1,0:T(8,128)(2,1)S(1)}, bf16[1,1,24,128,128]{4,3,2,1,0:T(8,128)(2,1)}, u32[]{:S(2)}) copy-start(bf16[1,1,24,128,128]{4,3,2,1,0:T(8,128)(2,1)} %param.10) | copy-start | bytes 2359300
  7.2 243.4 %all-reduce.5.cloned.1.call-start = ((), (), s32[]{:S(2)}) async-start(), calls=%async_computation.2 | async-start | bytes 1835008 | tf_op jit(solution)/shard_map/psum | solution.py:46
  32.5 2.0 copy-start.7
  36.7 308.8 %reduce-scatter.3.cloned.1.call-start = ((), (), s32[]{:S(2)}) async-start(), calls=%async_computation.3 | async-start | bytes 1114112 | tf_op jit(solution)/shard_map/reduce_scatter | solution.py:64
  255.0 2.0 copy-start.8
  258.0 193.6 %copy-start.6 = (f32[128]{0:T(128)S(1)}, f32[128]{0:T(128)}, u32[]{:S(2)}) copy-start(f32[128]{0:T(128)} %param.15) | copy-start | bytes 1540
  258.0 193.6 %copy-start.3 = (f32[128,128]{1,0:T(8,128)S(1)}, f32[128,128]{1,0:T(8,128)}, u32[]{:S(2)}) copy-start(f32[128,128]{1,0:T(8,128)} %param.14) | copy-start | bytes 196612
  259.3 423.9 %all-reduce.7.cloned.1.call-start = ((), (), s32[]{:S(2)}) async-start(), calls=%async_computation.4 | async-start | bytes 1835008 | tf_op jit(solution)/shard_map/psum | solution.py:46
  473.9 209.3 %copy-start.1 = (f32[1792,128]{1,0:T(8,128)S(1)}, f32[1792,128]{1,0:T(8,128)}, u32[]{:S(2)}) copy-start(f32[1792,128]{1,0:T(8,128)} %all-reduce.5.cloned.1.call-done) | copy-start | bytes 2752516
  475.1 406.3 %reduce-scatter.5.cloned.1.call-start = ((), (), s32[]{:S(2)}) async-start(), calls=%async_computation.5 | async-start | bytes 1114112 | tf_op jit(solution)/shard_map/reduce_scatter | solution.py:64
  683.2 106.7 %copy-start.2 = (f32[1792,128]{1,0:T(8,128)S(1)}, f32[1792,128]{1,0:T(8,128)}, u32[]{:S(2)}) copy-start(f32[1792,128]{1,0:T(8,128)} %all-reduce.7.cloned.1.call-done) | copy-start | bytes 2752516
  801.6 187.2 %copy-start.4 = (f32[128,128]{1,0:T(8,128)S(1)}, f32[128,128]{1,0:T(8,128)}, u32[]{:S(2)}) copy-start(f32[128,128]{1,0:T(8,128)} %reduce-scatter.3.cloned.1.call-done) | copy-start | bytes 196612
  881.4 107.4 %copy-start.5 = (f32[128,128]{1,0:T(8,128)S(1)}, f32[128,128]{1,0:T(8,128)}, u32[]{:S(2)}) copy-start(f32[128,128]{1,0:T(8,128)} %reduce-scatter.5.cloned.1.call-done) | copy-start | bytes 196612
Sparse Core Ops, SparseCore 0:
  36.8 213.6 all-reduce.4
  259.5 85.9 reduce-scatter.2
  475.3 207.9 all-reduce.6
  801.7 79.6 reduce-scatter.4
where the time goes:
time: 997 us; the launch traced here: 996 us
  waiting for transfers between devices  588 us (59%)
  blocking collectives  352 us (35%)
  local copies, waits for them, and re-layouts  17.6 us (2%)
  between operations  14.6 us (1%)
  matrix products  13.9 us (1%)
  other arithmetic  10.2 us (1%)
    psum x2, waiting for transfers between devices, reduce_grad(): return lax.psum(partial_contribution, 'comp')  422 us
    psum x2, blocking collectives, grad_total(): lax.psum(first_comp * jnp.sum(gradient * gradient, axis=0), ('comp', 'fea...  210 us
    reduce_scatter x2, waiting for transfers between devices, shards(): lax.psum_scatter(forward_summed.reshape(RB_DEV * block_edge, responses),...  166 us
    psum x1, blocking collectives, shards(): lax.psum((image_weight * jnp.sum(image_rows * image_rows, axis=0), first_...  105 us
    all_gather x2, blocking collectives, slab_of(): lax.all_gather(current.astype(jnp.bfloat16), 'feat', axis=0, tiled=True)  36 us
  transfers between devices with their start and end apart: 4, of which 4 were waited for; matrix products, arithmetic and copies ran while one was open for 0% of the time, Pallas kernels for 0%

commit v1 on v0

--- a/solution.py
+++ b/solution.py
@@ -6,6 +6,10 @@
 RB_DEV = 16
 CB_DEV = 14
 ITERS = 2
+
+
+def start_the_inputs(x_part):
+    return jnp.sum(lax.all_gather(x_part, ("comp", "feat")), axis=0)
 
 
 def shards(block_values, block_rows, block_cols, block_counts, right_side, ridge):
@@ -46,7 +50,7 @@
         return lax.psum(partial_contribution, "comp")
 
     def grad_total(gradient):
-        return lax.psum(first_comp * jnp.sum(gradient * gradient, axis=0), ("comp", "feat"))
+        return start_the_inputs(first_comp * jnp.sum(gradient * gradient, axis=0))
 
     gradient = reduce_grad(backward(slab_of(residual)))
     energy = grad_total(gradient)

time: 997 us -> 1160 us (1.16)
  blocking collectives: 352 us -> 598 us
  waiting for transfers between devices: 588 us -> 505 us
    all_gather x0 -> x2, blocking collectives: none -> 352 us  [start_the_inputs(): return jnp.sum(lax.all_gather(x_part, ('comp', 'feat')), axis=0)]
    psum x2 -> x0, blocking collectives: 210 us -> none  [grad_total(): lax.psum(first_comp * jnp.sum(gradient * gradient, axis=0), ('comp', 'fea...]
    psum x1 -> x2, blocking collectives: 105 us -> 209 us  [shards(): lax.psum((image_weight * jnp.sum(image_rows * image_rows, axis=0), first_...]
    reduce_scatter x2, waiting for transfers between devices: 166 us -> 85.1 us  [shards(): lax.psum_scatter(forward_summed.reshape(RB_DEV * block_edge, responses),...]
  transfers between devices with their start and end apart: 4 -> 4, of which waited for: 4 -> 3; matrix products, arithmetic and copies ran while one was open for 0% -> 0% of each run, Pallas kernels for 0% -> 0%
where the time goes in v1:
time: 1160 us
  blocking collectives  598 us (52%)
  waiting for transfers between devices  505 us (44%)
  local copies, waits for them, and re-layouts  17.6 us (2%)
  between operations  14.7 us (1%)
  matrix products  13.9 us (1%)
    psum x2, waiting for transfers between devices, reduce_grad(): return lax.psum(partial_contribution, 'comp')  420 us
    all_gather x2, blocking collectives, start_the_inputs(): return jnp.sum(lax.all_gather(x_part, ('comp', 'feat')), axis=0)  352 us
    psum x2, blocking collectives, shards(): lax.psum((image_weight * jnp.sum(image_rows * image_rows, axis=0), first_...  209 us
    reduce_scatter x2, waiting for transfers between devices, shards(): lax.psum_scatter(forward_summed.reshape(RB_DEV * block_edge, responses),...  85.1 us
    all_gather x2, blocking collectives, slab_of(): lax.all_gather(current.astype(jnp.bfloat16), 'feat', axis=0, tiled=True)  36.4 us
  transfers between devices with their start and end apart: 4, of which 3 were waited for; matrix products, arithmetic and copies ran while one was open for 0% of the time, Pallas kernels for 0%

profile of v1, /device:TPU:1, one launch (start us, length us, event | category | flops | bytes accessed | tf_op | source)
XLA Modules:
  0.0 1160.5 jit_solution(7649192751832702972)
XLA Ops:
  10.1 20.0 %all_gather.14 = bf16[2048,128]{1,0:T(8,128)(2,1)S(1)} all-gather(bf16[128,128]{1,0:T(8,128)(2,1)S(1)} %convert_element_type.26), channel_id=1, replica_groups=mesh['comp'=32,'feat'=16] {'feat'}, dimensions={0}, use_global_device_ids=true | all-gather | bytes 557056 | tf_op jit(solution)/shard_map/all_gather | solution.py:47
  30.8 1.7 convolution_bitcast_fusion.3
  32.5 2.0 copy.21
  35.5 1.2 copy.22
  36.8 213.7 %all-reduce.5.cloned.1.call-done = f32[1792,128]{1,0:T(8,128)} async-done(((f32[1792,128]{1,0:T(8,128)}), f32[1792,128]{1,0:T(8,128)}) %all-reduce.5.cloned.1.call-update) | async-done | bytes 917520 | tf_op jit(solution)/shard_map/psum | solution.py:50
  250.5 1.7 multiply_reduce_fusion.2
  253.0 2.0 convolution_bitcast_fusion.2
  255.0 2.0 copy.24
  258.0 1.3 copy.25
  259.4 179.0 %all-gather.2 = f32[512,1,128]{2,1,0:T(1,128)S(1)} all-gather(f32[1,1,128]{2,1,0:T(1,128)S(1)} %fusion.54), channel_id=2, replica_groups=mesh['comp'=32,'feat'=16] {'comp','feat'}, dimensions={0}, use_global_device_ids=true | all-gather | bytes 262656 | tf_op jit(solution)/shard_map/all_gather | solution.py:12
  439.9 103.6 %all-reduce.1 = (f32[128]{0:T(128)S(1)}, f32[128]{0:T(128)S(1)}) all-reduce(f32[128]{0:T(128)S(1)} %multiply_reduce_fusion.4, f32[128]{0:T(128)S(1)} %broadcast_multiply_fusion.1), channel_id=1, replica_groups=mesh['comp'=32,'feat'=16] {'comp','feat'}, use_global_device_ids=true, to_apply=%region_5.8 | all-reduce | flops 256 | bytes 2048 | tf_op jit(solution)/shard_map/psum | solution.py:74
  544.3 16.4 %all_gather.16 = bf16[2048,128]{1,0:T(8,128)(2,1)S(1)} all-gather(bf16[128,128]{1,0:T(8,128)(2,1)S(1)} %fusion.16), channel_id=1, replica_groups=mesh['comp'=32,'feat'=16] {'feat'}, dimensions={0}, use_global_device_ids=true | all-gather | bytes 557056 | tf_op jit(solution)/shard_map/all_gather | solution.py:47
  561.5 1.7 convolution_bitcast_fusion.1
  563.1 2.0 copy.27
  567.4 206.2 %all-reduce.7.cloned.1.call-done = f32[1792,128]{1,0:T(8,128)} async-done(((f32[1792,128]{1,0:T(8,128)}), f32[1792,128]{1,0:T(8,128)}) %all-reduce.7.cloned.1.call-update) | async-done | bytes 917520 | tf_op jit(solution)/shard_map/psum | solution.py:50
  773.6 1.5 multiply_reduce_fusion.1
  775.1 173.3 %all-gather.3 = f32[512,1,128]{2,1,0:T(1,128)S(1)} all-gather(f32[1,1,128]{2,1,0:T(1,128)S(1)} %multiply_bitcast_fusion), channel_id=3, replica_groups=mesh['comp'=32,'feat'=16] {'comp','feat'}, dimensions={0}, use_global_device_ids=true | all-gather | bytes 262656 | tf_op jit(solution)/shard_map/all_gather | solution.py:12
  949.3 1.6 gather_fusion.3
  950.8 3.1 convolution_bitcast_fusion
  954.0 3.0 copy.30
  957.0 2.4 fusion.17
  959.4 1.3 copy.31
  960.8 85.1 %reduce-scatter.5.cloned.1.call-done = f32[128,128]{1,0:T(8,128)} async-done(((f32[2048,128]{1,0:T(8,128)}), f32[128,128]{1,0:T(8,128)}) %reduce-scatter.5.cloned.1.call-update) | async-done | bytes 65552 | tf_op jit(solution)/shard_map/reduce_scatter | solution.py:68
  1046.8 105.3 %all-reduce = (f32[128]{0:T(128)S(1)}, f32[128]{0:T(128)S(1)}) all-reduce(f32[128]{0:T(128)S(1)} %multiply_reduce_fusion.3, f32[128]{0:T(128)S(1)} %broadcast_multiply_fusion), channel_id=1, replica_groups=mesh['comp'=32,'feat'=16] {'comp','feat'}, use_global_device_ids=true, to_apply=%region_12.15 | all-reduce | flops 256 | bytes 2048 | tf_op jit(solution)/shard_map/psum | solution.py:74
  (57 shorter events, 14.8 us)
Async XLA Ops:
  7.2 23.6 %copy-start = (bf16[1,1,24,128,128]{4,3,2,1,0:T(8,128)(2,1)S(1)}, bf16[1,1,24,128,128]{4,3,2,1,0:T(8,128)(2,1)}, u32[]{:S(2)}) copy-start(bf16[1,1,24,128,128]{4,3,2,1,0:T(8,128)(2,1)} %param.10) | copy-start | bytes 2359300
  7.2 243.4 %all-reduce.5.cloned.1.call-start = ((), (), s32[]{:S(2)}) async-start(), calls=%async_computation.2 | async-start | bytes 1835008 | tf_op jit(solution)/shard_map/psum | solution.py:50
  32.5 2.0 copy-start.7
  36.7 402.3 %reduce-scatter.3.cloned.1.call-start = ((), (), s32[]{:S(2)}) async-start(), calls=%async_computation.3 | async-start | bytes 1114112 | tf_op jit(solution)/shard_map/reduce_scatter | solution.py:68
  255.0 2.0 copy-start.8
  258.0 285.5 %copy-start.6 = (f32[128]{0:T(128)S(1)}, f32[128]{0:T(128)}, u32[]{:S(2)}) copy-start(f32[128]{0:T(128)} %param.15) | copy-start | bytes 1540
  258.0 285.5 %copy-start.3 = (f32[128,128]{1,0:T(8,128)S(1)}, f32[128,128]{1,0:T(8,128)}, u32[]{:S(2)}) copy-start(f32[128,128]{1,0:T(8,128)} %param.14) | copy-start | bytes 196612
  259.3 514.2 %all-reduce.7.cloned.1.call-start = ((), (), s32[]{:S(2)}) async-start(), calls=%async_computation.4 | async-start | bytes 1835008 | tf_op jit(solution)/shard_map/psum | solution.py:50
  566.1 207.5 %copy-start.1 = (f32[1792,128]{1,0:T(8,128)S(1)}, f32[1792,128]{1,0:T(8,128)}, u32[]{:S(2)}) copy-start(f32[1792,128]{1,0:T(8,128)} %all-reduce.5.cloned.1.call-done) | copy-start | bytes 2752516
  567.3 478.5 %reduce-scatter.5.cloned.1.call-start = ((), (), s32[]{:S(2)}) async-start(), calls=%async_computation.5 | async-start | bytes 1114112 | tf_op jit(solution)/shard_map/reduce_scatter | solution.py:68
  773.6 175.4 %copy-start.2 = (f32[1792,128]{1,0:T(8,128)S(1)}, f32[1792,128]{1,0:T(8,128)}, u32[]{:S(2)}) copy-start(f32[1792,128]{1,0:T(8,128)} %all-reduce.7.cloned.1.call-done) | copy-start | bytes 2752516
  960.7 192.5 %copy-start.4 = (f32[128,128]{1,0:T(8,128)S(1)}, f32[128,128]{1,0:T(8,128)}, u32[]{:S(2)}) copy-start(f32[128,128]{1,0:T(8,128)} %reduce-scatter.3.cloned.1.call-done) | copy-start | bytes 196612
  1045.9 107.4 %copy-start.5 = (f32[128,128]{1,0:T(8,128)S(1)}, f32[128,128]{1,0:T(8,128)}, u32[]{:S(2)}) copy-start(f32[128,128]{1,0:T(8,128)} %reduce-scatter.5.cloned.1.call-done) | copy-start | bytes 196612
Sparse Core Ops, SparseCore 0:
  36.8 213.6 all-reduce.4
  259.5 85.9 reduce-scatter.2
  567.5 206.0 all-reduce.6
  960.9 84.9 reduce-scatter.4
